TPU v7x, 256 devices: a whole 4x4x8 slice. The times are simulated.
256 devices in a mesh: dp: 32 (over x, z), own: 8 (over y, core).
Axes of the slice: x: 4, y: 4, z: 8, core: 2. Of those that a mesh axis runs over, the one named last changes fastest.
Arguments:
- partials: bfloat16 [32, 64, 256, 1024], P('dp', None, None, 'own')
- owner: int32 [64, 1], replicated, may hold values from 0 to 31; in each aligned block of 64 rows (0 to 63, 64 to 127, ...) at most 4 rows name the same one
- momentum: float32 [32, 4, 256, 1024], P('dp', None, None, 'own'), may hold values from -1.2 to 1.2
- master: float32 [32, 4, 256, 1024], P('dp', None, None, 'own'), may hold values from -0.3 to 0.3
Outputs:
- new_momentum: float32 [32, 4, 256, 1024], P('dp', None, None, 'own')
- new_master: float32 [32, 4, 256, 1024], P('dp', None, None, 'own')
- new_weights: bfloat16 [64, 256, 1024], P(None, None, 'own')
Inputs may be any that keep to these rules, and one draw needn't show every extreme that they name: `owner`: every group owns at least one block and at most 4 blocks; some group owns exactly 4.
All inputs are finite; a program needn't handle non-finite values.
Results may differ from a plain program's by a relative error of at most 0.0007.
Values may be sent and summed in bfloat16 or wider, within the bound.
No kernel may reach another device: no remote copies, remote signals or barrier semaphores. Data moves between devices by JAX's collectives and lax.ppermute only.
A program may use at most 128 MiB of HBM per device.

v0:
```python
import math
import jax
import jax.numpy as jnp
from jax import lax
from jax.sharding import PartitionSpec as P

D = 1024
ITERS = 5
COEF_A = 3.4445
COEF_B = -4.775
COEF_C = 2.0315
BETA = 0.95
STEP_SIZE = 0.2
DECAY = 0.1
EPSILON = 1e-07


def slot_targets(owner_list, group_count, slot_count):
    onehot = (owner_list[:, None] == jnp.arange(group_count, dtype=jnp.int32)[None, :]).astype(
        jnp.int32
    )
    before = jnp.cumsum(onehot, axis=0) - onehot
    ranks = jnp.sum(before * onehot, axis=1)
    return owner_list * slot_count + ranks


def slot_sources(target, slot_count, block_count):
    positions = jnp.arange(slot_count, dtype=jnp.int32)
    matches = positions[:, None] == target[None, :]
    present = jnp.any(matches, axis=1)
    source = jnp.sum(
        jnp.where(matches, jnp.arange(block_count, dtype=jnp.int32)[None, :], 0), axis=1
    )
    return (present, source)


def local_gram(values):
    return jnp.einsum(
        "srk,stk->srt",
        values,
        values,
        precision=lax.Precision.HIGHEST,
        preferred_element_type=jnp.float32,
    )


def gram_total(values):
    return lax.psum(local_gram(values), "own")


def matmul(left, right):
    return jnp.einsum(
        "srt,stu->sru",
        left,
        right,
        precision=lax.Precision.HIGHEST,
        preferred_element_type=jnp.float32,
    )


def newton_turn(ortho, gram, eye, next_gram):
    square = matmul(gram, gram)
    poly = COEF_B * gram + COEF_C * square
    product = jnp.einsum(
        "srt,stk->srk",
        poly,
        ortho,
        precision=lax.Precision.HIGHEST,
        preferred_element_type=jnp.float32,
    )
    ortho = COEF_A * ortho + product
    if next_gram:
        step = COEF_A * eye + poly
        gram = matmul(step, matmul(gram, step))
    return (ortho, gram)


def on_device(partials, owner, momentum, master):
    group_count = lax.axis_size("dp")
    local_rows = partials[0]
    block_count = local_rows.shape[0]
    slot_count = momentum.shape[1]
    block_rows = momentum.shape[2]
    owner_list = owner[:, 0]
    target = slot_targets(owner_list, group_count, slot_count)
    present, source = slot_sources(target, group_count * slot_count, block_count)
    outgoing = jnp.where(
        present[:, None, None], jnp.take(local_rows, source, axis=0).astype(jnp.float32), 0.0
    )
    gradient = lax.psum_scatter(outgoing, "dp", scatter_dimension=0, tiled=True)
    momentum_new = BETA * momentum[0] + gradient
    update = gradient + BETA * momentum_new
    update_gram = gram_total(update)
    squares = jnp.trace(update_gram, axis1=1, axis2=2)
    factor = 1.0 / (jnp.sqrt(squares) + EPSILON)
    ortho = update * factor[:, None, None]
    gram = update_gram * (factor * factor)[:, None, None]
    eye = jnp.eye(block_rows, dtype=jnp.float32)[None]
    for iteration in range(ITERS):
        ortho, gram = newton_turn(ortho, gram, eye, iteration < ITERS - 1)
    step_factor = STEP_SIZE * 0.2 * math.sqrt(max(block_rows, D))
    master_new = master[0] * (1.0 - STEP_SIZE * DECAY) - step_factor * ortho
    weights_low = master_new.astype(jnp.bfloat16)
    every_slot = lax.all_gather(weights_low, "dp", axis=0, tiled=True)
    weights = jnp.take(every_slot, target, axis=0)
    return (momentum_new[None], master_new[None], weights)


def solution(mesh):
    in_specs = (
        P("dp", None, None, "own"),
        P(),
        P("dp", None, None, "own"),
        P("dp", None, None, "own"),
    )
    out_specs = (P("dp", None, None, "own"), P("dp", None, None, "own"), P(None, None, "own"))
    return jax.shard_map(
        on_device, mesh=mesh, in_specs=in_specs, out_specs=out_specs, check_vma=False
    )
```

profile of v0, /device:TPU:1, one launch (start us, length us, event | category | flops | bytes accessed | tf_op | source)
XLA Modules:
  0.0 493.5 jit_solution(1865720809806670317)
XLA Ops:
  7.2 0.0 reduce-scatter.2.cloned.1.call-start
  7.2 0.7 fusion.39
  7.9 0.1 reduce_window_sum.11
  8.0 0.8 select_reduce_fusion.2
  8.9 0.7 multiply_add_fusion.3
  9.5 0.1 select_reduce_fusion.1
  9.7 0.1 fusion.40
  9.8 8.6 %gather_fusion = bf16[128,256,128]{2,1,0:T(8,128)(2,1)} fusion(bf16[64,256,128]{2,1,0:T(8,128)(2,1)} %bitcast.57, s32[1024]{0:T(1024)S(1)} %pad_clamp_fusion.1), kind=kCustom, calls=%fused_computation | custom fusion | bytes 16777728 | tf_op jit(solution)/shard_map/jit(_take)/gather | solution.py:88
  18.4 13.4 %convert_select_fusion = f32[128,256,128]{2,1,0:T(8,128)} fusion(bf16[128,256,128]{2,1,0:T(8,128)(2,1)} %gather_fusion, pred[128]{0:T(512)(128)(4,1)S(1)} %compare_and_fusion, pred[128]{0:T(512)(128)(4,1)S(1)} %fusion.40), kind=kLoop, calls=%fused_computation.2 | loop fusion | flops 12582912 | bytes 25166080 | tf_op jit(solution)/shard_map/jit(_where)/select_n | solution.py:87
  31.7 0.0 copy-start
  31.7 0.0 reduce-scatter.2.cloned.1.call-update
  31.8 0.0 all-reduce.2.cloned.1.call-start
  31.8 245.8 %reduce-scatter.2.cloned.1.call-done = f32[4,256,128]{2,1,0:T(8,128)} async-done(((f32[128,256,128]{2,1,0:T(8,128)}), f32[4,256,128]{2,1,0:T(8,128)}) %reduce-scatter.2.cloned.1.call-update) | async-done | bytes 524304 | tf_op jit(solution)/shard_map/reduce_scatter | solution.py:90
  277.7 0.0 copy-done
  277.7 3.3 fusion.38
  280.9 0.0 all-reduce.2.cloned.1.call-update
  281.0 0.2 all-gather.2.cloned.1.call-start
  281.2 0.0 copy-start.1
  281.3 68.5 %all-reduce.2.cloned.1.call-done = f32[4,256,256]{2,1,0:T(8,128)} async-done(((f32[4,256,256]{2,1,0:T(8,128)}), f32[4,256,256]{2,1,0:T(8,128)}) %all-reduce.2.cloned.1.call-update) | async-done | bytes 1048592 | tf_op jit(solution)/shard_map/psum | solution.py:48
  349.7 1.4 select_reduce_fusion
  351.2 3.4 fusion.4
  354.6 2.5 fusion.21
  357.1 1.2 fusion.19
  358.3 1.3 fusion.3
  359.6 1.2 fusion.17
  360.8 0.0 copy-done.1
  360.8 1.2 convolution_add_fusion.4
  362.0 1.1 convolution_add_fusion.3
  363.0 1.2 fusion.15
  364.2 1.3 fusion.2
  365.5 1.4 fusion.13
  366.9 1.1 convolution_add_fusion.2
  368.0 1.2 fusion.11
  369.2 0.0 copy-start.2
  369.2 1.3 fusion.1
  370.5 0.0 copy-start.3
  370.5 1.2 fusion.9
  371.7 1.1 convolution_add_fusion.1
  372.8 1.2 fusion.7
  374.0 1.3 fusion
  375.3 0.0 copy-done.2
  375.3 2.0 fusion.45
  377.3 0.0 all-gather.2.cloned.1.call-update
  377.3 0.0 copy-done.3
  377.3 0.9 fusion.36
  378.2 97.7 %all-gather.2.cloned.1.call-done = bf16[128,256,128]{2,1,0:T(8,128)(2,1)} async-done(((bf16[4,256,128]{2,1,0:T(8,128)(2,1)}), bf16[128,256,128]{2,1,0:T(8,128)(2,1)}) %all-gather.2.cloned.1.call-update) | async-done | bytes 8388624 | tf_op jit(solution)/shard_map/all_gather | solution.py:104
  475.9 6.5 %gather_fusion.1 = bf16[64,256,128]{2,1,0:T(8,128)(2,1)} fusion(bf16[128,256,128]{2,1,0:T(8,128)(2,1)} %all-gather.2.cloned.1.call-done, s32[1024]{0:T(1024)S(1)} %pad_clamp_fusion), kind=kCustom, calls=%fused_computation.1 | custom fusion | bytes 8388864 | tf_op jit(solution)/shard_map/jit(_take)/gather | solution.py:105
  482.4 4.6 broadcast_select_fusion
  (8 shorter events, 0.1 us)
Async XLA Ops:
  7.2 270.5 %reduce-scatter.2.cloned.1.call-start = ((), (), s32[]{:S(2)}) async-start(), calls=%async_computation.1 | async-start | bytes 17301504 | tf_op jit(solution)/shard_map/reduce_scatter | solution.py:90
  31.7 245.9 %copy-start = (f32[1,4,256,128]{3,2,1,0:T(8,128)S(1)}, f32[1,4,256,128]{3,2,1,0:T(8,128)}, u32[]{:S(2)}) copy-start(f32[1,4,256,128]{3,2,1,0:T(8,128)} %param.6) | copy-start | bytes 1572868
  31.8 318.0 %all-reduce.2.cloned.1.call-start = ((), (), s32[]{:S(2)}) async-start(), calls=%async_computation.2 | async-start | bytes 2097152 | tf_op jit(solution)/shard_map/psum | solution.py:48
  281.0 194.9 %all-gather.2.cloned.1.call-start = ((), (), s32[]{:S(2)}) async-start(), calls=%async_computation.3 | async-start | bytes 8650752 | tf_op jit(solution)/shard_map/all_gather | solution.py:104
  281.2 79.5 %copy-start.1 = (f32[4,256,128]{2,1,0:T(8,128)S(1)}, f32[4,256,128]{2,1,0:T(8,128)}, u32[]{:S(2)}) copy-start(f32[4,256,128]{2,1,0:T(8,128)} %reduce-scatter.2.cloned.1.call-done) | copy-start | bytes 1572868
  369.2 6.1 %copy-start.2 = (f32[1,4,256,128]{3,2,1,0:T(8,128)S(1)}, f32[1,4,256,128]{3,2,1,0:T(8,128)}, u32[]{:S(2)}) copy-start(f32[1,4,256,128]{3,2,1,0:T(8,128)} %param.7) | copy-start | bytes 1572868
  370.5 6.8 %copy-start.3 = (s32[64,1]{0,1:T(1,128)S(1)}, s32[64,1]{0,1:T(1,128)}, u32[]{:S(2)}) copy-start(s32[64,1]{0,1:T(1,128)} %param.5) | copy-start | bytes 772
Sparse Core Ops, SparseCore 0:
  31.9 245.7 reduce-scatter.1
  281.1 68.5 all-reduce.1
  377.4 98.4 all-gather.1
where the time goes:
time: 494 us
  waiting for transfers between devices  412 us (83%)
  matrix products  29.2 us (6%)
  other arithmetic  22.9 us (5%)
  local copies, waits for them, and re-layouts  15.1 us (3%)
  between operations  14 us (3%)
    reduce_scatter x1, waiting for transfers between devices, on_device(): gradient = lax.psum_scatter(outgoing, 'dp', scatter_dimension=0, tiled=True)  246 us
    all_gather x1, waiting for transfers between devices, on_device(): every_slot = lax.all_gather(weights_low, 'dp', axis=0, tiled=True)  97.7 us
    psum x1, waiting for transfers between devices, gram_total(): return lax.psum(local_gram(values), 'own')  68.5 us
    dot_general x13, matrix products, matmul(): jnp.einsum('srt,stu->sru', left, right, precision=lax.Precision.HIGHEST,...  19.5 us
    select_n x1, other arithmetic, on_device(): jnp.where(present[:, None, None], jnp.take(local_rows, source, axis=0).as...  13.4 us
  transfers between devices with their start and end apart: 3, of which 3 were waited for; matrix products, arithmetic and copies ran while one was open for 0% of the time, Pallas kernels for 0%

commit v1 on v0

--- a/solution.py
+++ b/solution.py
@@ -101,7 +101,9 @@
     step_factor = STEP_SIZE * 0.2 * math.sqrt(max(block_rows, D))
     master_new = master[0] * (1.0 - STEP_SIZE * DECAY) - step_factor * ortho
     weights_low = master_new.astype(jnp.bfloat16)
-    every_slot = lax.all_gather(weights_low, "dp", axis=0, tiled=True)
+    every_slot = jnp.concatenate(
+        lax.all_to_all(jnp.stack([weights_low] * lax.axis_size("dp")), "dp", 0, 0), axis=0
+    )
     weights = jnp.take(every_slot, target, axis=0)
     return (momentum_new[None], master_new[None], weights)
 

time: 494 us -> 613 us (1.24)
  the two profiles are of different devices: /device:TPU:1 before, /device:TPU:123 now
where the time goes in v1:
time: 613 us
  waiting for transfers between devices  516 us (84%)
  matrix products  29.1 us (5%)
  other arithmetic  22.9 us (4%)
  local copies, waits for them, and re-layouts  20.4 us (3%)
  between operations  14.3 us (2%)
  starting transfers between devices  9.75 us (2%)
    reduce_scatter x1, waiting for transfers between devices, on_device(): gradient = lax.psum_scatter(outgoing, 'dp', scatter_dimension=0, tiled=True)  242 us
    all_to_all x1, waiting for transfers between devices, on_device(): lax.all_to_all(jnp.stack([weights_low] * lax.axis_size('dp')), 'dp', 0, 0)  203 us
    psum x1, waiting for transfers between devices, gram_total(): return lax.psum(local_gram(values), 'own')  71.2 us
    dot_general x13, matrix products, matmul(): jnp.einsum('srt,stu->sru', left, right, precision=lax.Precision.HIGHEST,...  19.5 us
    select_n x1, other arithmetic, on_device(): jnp.where(present[:, None, None], jnp.take(local_rows, source, axis=0).as...  13.4 us
  transfers between devices with their start and end apart: 3, of which 3 were waited for; matrix products, arithmetic and copies ran while one was open for 0% of the time, Pallas kernels for 0%

profile of v1, /device:TPU:123, one launch (start us, length us, event | category | flops | bytes accessed | tf_op | source)
XLA Modules:
  0.0 612.6 jit_solution(17633158714084922669)
XLA Ops:
  7.2 0.0 reduce-scatter.2.cloned.1.call-start
  7.2 0.7 fusion.39
  7.9 0.1 reduce_window_sum.11
  8.0 0.8 select_reduce_fusion.2
  8.9 0.7 multiply_add_fusion.3
  9.5 0.1 select_reduce_fusion.1
  9.7 0.1 fusion.40
  9.8 8.6 %gather_fusion = bf16[128,256,128]{2,1,0:T(8,128)(2,1)} fusion(bf16[64,256,128]{2,1,0:T(8,128)(2,1)} %bitcast.58, s32[1024]{0:T(1024)S(1)} %pad_clamp_fusion.1), kind=kCustom, calls=%fused_computation | custom fusion | bytes 16777728 | tf_op jit(solution)/shard_map/jit(_take)/gather | solution.py:88
  18.4 13.4 %convert_select_fusion = f32[128,256,128]{2,1,0:T(8,128)} fusion(bf16[128,256,128]{2,1,0:T(8,128)(2,1)} %gather_fusion, pred[128]{0:T(512)(128)(4,1)S(1)} %compare_and_fusion, pred[128]{0:T(512)(128)(4,1)S(1)} %fusion.40), kind=kLoop, calls=%fused_computation.2 | loop fusion | flops 12582912 | bytes 25166080 | tf_op jit(solution)/shard_map/jit(_where)/select_n | solution.py:87
  31.7 0.0 copy-start
  31.7 0.0 reduce-scatter.2.cloned.1.call-update
  31.8 0.2 all-reduce.2.cloned.1.call-start
  32.0 241.8 %reduce-scatter.2.cloned.1.call-done = f32[4,256,128]{2,1,0:T(8,128)} async-done(((f32[128,256,128]{2,1,0:T(8,128)}), f32[4,256,128]{2,1,0:T(8,128)}) %reduce-scatter.2.cloned.1.call-update) | async-done | bytes 524304 | tf_op jit(solution)/shard_map/reduce_scatter | solution.py:90
  273.8 0.0 copy-done
  273.8 3.3 fusion.38
  277.1 0.0 all-reduce.2.cloned.1.call-update
  277.1 0.0 copy-start.1
  277.2 71.2 %all-reduce.2.cloned.1.call-done = f32[4,256,256]{2,1,0:T(8,128)} async-done(((f32[4,256,256]{2,1,0:T(8,128)}), f32[4,256,256]{2,1,0:T(8,128)}) %all-reduce.2.cloned.1.call-update) | async-done | bytes 1048592 | tf_op jit(solution)/shard_map/psum | solution.py:48
  348.4 1.4 select_reduce_fusion
  349.8 3.4 fusion.4
  353.3 2.5 fusion.21
  355.7 1.2 fusion.19
  356.9 1.3 fusion.3
  358.2 1.2 fusion.17
  359.4 0.0 copy-done.1
  359.4 1.2 convolution_add_fusion.4
  360.6 1.1 convolution_add_fusion.3
  361.7 1.2 fusion.15
  362.9 1.5 fusion.2
  364.4 1.2 fusion.13
  365.6 1.1 convolution_add_fusion.2
  366.7 1.2 fusion.11
  367.9 0.0 copy-start.2
  367.9 1.3 fusion.1
  369.2 1.2 fusion.9
  370.4 1.1 convolution_add_fusion.1
  371.4 1.2 fusion.7
  372.6 1.3 fusion
  373.9 0.0 copy-done.2
  373.9 1.9 fusion.45
  375.8 5.3 stack.2
  381.1 0.0 copy-start.3
  381.1 9.5 %all-to-all-start = ((bf16[32,4,256,128]{3,2,1,0:T(8,128)(2,1)}), bf16[32,4,256,128]{3,2,1,0:T(8,128)(2,1)}, u32[]{:S(2)}, u32[]{:S(2)}) async-start(bf16[32,4,256,128]{3,2,1,0:T(8,128)(2,1)} %stack.2), calls=%async_computation.1 | async-start | bytes 16777216 | tf_op jit(solution)/shard_map/all_to_all | solution.py:105
  390.6 0.0 copy-done.3
  390.7 0.9 fusion.36
  391.5 203.1 %all-to-all-done = bf16[32,4,256,128]{3,2,1,0:T(8,128)(2,1)} async-done(((bf16[32,4,256,128]{3,2,1,0:T(8,128)(2,1)}), bf16[32,4,256,128]{3,2,1,0:T(8,128)(2,1)}, u32[]{:S(2)}, u32[]{:S(2)}) %all-to-all-start) | async-done | bytes 8388640 | tf_op jit(solution)/shard_map/all_to_all | solution.py:105
  594.6 6.5 %gather_fusion.1 = bf16[64,256,128]{2,1,0:T(8,128)(2,1)} fusion(bf16[128,256,128]{2,1,0:T(8,128)(2,1)} %bitcast.10, s32[1024]{0:T(1024)S(1)} %pad_clamp_fusion), kind=kCustom, calls=%fused_computation.1 | custom fusion | bytes 8388864 | tf_op jit(solution)/shard_map/jit(_take)/gather | solution.py:107
  601.1 4.6 broadcast_select_fusion
  (8 shorter events, 0.1 us)
Async XLA Ops:
  7.2 266.6 %reduce-scatter.2.cloned.1.call-start = ((), (), s32[]{:S(2)}) async-start(), calls=%async_computation.2 | async-start | bytes 17301504 | tf_op jit(solution)/shard_map/reduce_scatter | solution.py:90
  31.7 242.1 %copy-start = (f32[1,4,256,128]{3,2,1,0:T(8,128)S(1)}, f32[1,4,256,128]{3,2,1,0:T(8,128)}, u32[]{:S(2)}) copy-start(f32[1,4,256,128]{3,2,1,0:T(8,128)} %param.6) | copy-start | bytes 1572868
  31.8 316.6 %all-reduce.2.cloned.1.call-start = ((), (), s32[]{:S(2)}) async-start(), calls=%async_computation.3 | async-start | bytes 2097152 | tf_op jit(solution)/shard_map/psum | solution.py:48
  277.1 82.3 %copy-start.1 = (f32[4,256,128]{2,1,0:T(8,128)S(1)}, f32[4,256,128]{2,1,0:T(8,128)}, u32[]{:S(2)}) copy-start(f32[4,256,128]{2,1,0:T(8,128)} %reduce-scatter.2.cloned.1.call-done) | copy-start | bytes 1572868
  367.9 6.0 copy-start.2
  381.1 9.5 %copy-start.3 = (s32[64,1]{0,1:T(1,128)S(1)}, s32[64,1]{0,1:T(1,128)}, u32[]{:S(2)}) copy-start(s32[64,1]{0,1:T(1,128)} %param.5) | copy-start | bytes 772
  381.1 213.5 %all-to-all-start = ((bf16[32,4,256,128]{3,2,1,0:T(8,128)(2,1)}), bf16[32,4,256,128]{3,2,1,0:T(8,128)(2,1)}, u32[]{:S(2)}, u32[]{:S(2)}) async-start(bf16[32,4,256,128]{3,2,1,0:T(8,128)(2,1)} %stack.2), calls=%async_computation.1 | async-start | bytes 16777216 | tf_op jit(solution)/shard_map/all_to_all | solution.py:105
Sparse Core Ops, SparseCore 0:
  31.9 241.8 reduce-scatter.1
  277.2 71.1 all-reduce.1

commit v2 on v0

--- a/solution.py
+++ b/solution.py
@@ -45,7 +45,7 @@
 
 
 def gram_total(values):
-    return lax.psum(local_gram(values), "own")
+    return jnp.sum(lax.all_gather(local_gram(values), "own"), axis=0)
 
 
 def matmul(left, right):

time: 494 us -> 479 us (0.970)
  waiting for transfers between devices: 412 us -> 397 us
    psum x1 -> x0, waiting for transfers between devices: 68.5 us -> none  [gram_total(): return lax.psum(local_gram(values), 'own')]
    all_gather x0 -> x1, waiting for transfers between devices: none -> 55.3 us  [gram_total(): return jnp.sum(lax.all_gather(local_gram(values), 'own'), axis=0)]
where the time goes in v2:
time: 479 us; the launch traced here: 478 us
  waiting for transfers between devices  397 us (83%)
  matrix products  25.9 us (5%)
  other arithmetic  25.8 us (5%)
  local copies, waits for them, and re-layouts  15.1 us (3%)
  between operations  14 us (3%)
    reduce_scatter x1, waiting for transfers between devices, on_device(): gradient = lax.psum_scatter(outgoing, 'dp', scatter_dimension=0, tiled=True)  246 us
    all_gather x1, waiting for transfers between devices, on_device(): every_slot = lax.all_gather(weights_low, 'dp', axis=0, tiled=True)  96.1 us
    all_gather x1, waiting for transfers between devices, gram_total(): return jnp.sum(lax.all_gather(local_gram(values), 'own'), axis=0)  55.3 us
    dot_general x13, matrix products, matmul(): jnp.einsum('srt,stu->sru', left, right, precision=lax.Precision.HIGHEST,...  16.3 us
    select_n x1, other arithmetic, on_device(): jnp.where(present[:, None, None], jnp.take(local_rows, source, axis=0).as...  13.4 us
  transfers between devices with their start and end apart: 3, of which 3 were waited for; matrix products, arithmetic and copies ran while one was open for 0% of the time, Pallas kernels for 0%

profile of v2, /device:TPU:1, one launch (start us, length us, event | category | flops | bytes accessed | tf_op | source)
XLA Modules:
  0.0 478.4 jit_solution(17182615396338760026)
XLA Ops:
  7.2 0.0 reduce-scatter.2.cloned.1.call-start
  7.2 0.7 fusion.39
  7.9 0.1 reduce_window_sum.11
  8.0 0.8 select_reduce_fusion.2
  8.9 0.7 multiply_add_fusion.3
  9.5 0.1 select_reduce_fusion.1
  9.7 0.1 fusion.40
  9.8 8.6 %gather_fusion = bf16[128,256,128]{2,1,0:T(8,128)(2,1)} fusion(bf16[64,256,128]{2,1,0:T(8,128)(2,1)} %bitcast.58, s32[1024]{0:T(1024)S(1)} %pad_clamp_fusion.1), kind=kCustom, calls=%fused_computation | custom fusion | bytes 16777728 | tf_op jit(solution)/shard_map/jit(_take)/gather | solution.py:88
  18.4 13.4 %convert_select_fusion = f32[128,256,128]{2,1,0:T(8,128)} fusion(bf16[128,256,128]{2,1,0:T(8,128)(2,1)} %gather_fusion, pred[128]{0:T(512)(128)(4,1)S(1)} %compare_and_fusion, pred[128]{0:T(512)(128)(4,1)S(1)} %fusion.40), kind=kLoop, calls=%fused_computation.2 | loop fusion | flops 12582912 | bytes 25166080 | tf_op jit(solution)/shard_map/jit(_where)/select_n | solution.py:87
  31.7 0.0 reduce-scatter.2.cloned.1.call-update
  31.8 0.0 all-gather.6.cloned.1.call-start
  31.8 245.8 %reduce-scatter.2.cloned.1.call-done = f32[4,256,128]{2,1,0:T(8,128)} async-done(((f32[128,256,128]{2,1,0:T(8,128)}), f32[4,256,128]{2,1,0:T(8,128)}) %reduce-scatter.2.cloned.1.call-update) | async-done | bytes 524304 | tf_op jit(solution)/shard_map/reduce_scatter | solution.py:90
  277.7 0.0 copy-done
  277.7 3.3 fusion.38
  280.9 0.0 all-gather.6.cloned.1.call-update
  281.0 0.2 all-gather.4.cloned.1.call-start
  281.3 55.3 %all-gather.6.cloned.1.call-done = f32[32,256,256]{2,1,0:T(8,128)} async-done(((f32[4,256,256]{2,1,0:T(8,128)}), f32[32,256,256]{2,1,0:T(8,128)}) %all-gather.6.cloned.1.call-update) | async-done | bytes 8388624 | tf_op jit(solution)/shard_map/all_gather | solution.py:48
  336.6 4.1 reduce_sum.44
  340.6 0.0 copy-start.1
  340.6 0.2 select_reduce_fusion
  340.9 1.4 fusion.4
  342.3 1.2 fusion.21
  343.5 1.2 fusion.19
  344.7 1.3 fusion.3
  346.0 1.2 fusion.17
  347.2 0.0 copy-done.1
  347.2 1.2 convolution_add_fusion.4
  348.4 1.1 convolution_add_fusion.3
  349.5 1.2 fusion.15
  350.7 1.3 fusion.2
  352.0 1.4 fusion.13
  353.4 1.1 convolution_add_fusion.2
  354.5 1.2 fusion.11
  355.6 0.0 copy-start.2
  355.7 1.3 fusion.1
  356.9 0.0 copy-start.3
  357.0 1.2 fusion.9
  358.1 1.1 convolution_add_fusion.1
  359.2 1.2 fusion.7
  360.4 1.3 fusion
  361.7 0.0 copy-done.2
  361.7 2.0 fusion.45
  363.7 0.0 all-gather.4.cloned.1.call-update
  363.7 0.0 copy-done.3
  363.8 0.9 fusion.36
  364.6 96.1 %all-gather.4.cloned.1.call-done = bf16[128,256,128]{2,1,0:T(8,128)(2,1)} async-done(((bf16[4,256,128]{2,1,0:T(8,128)(2,1)}), bf16[128,256,128]{2,1,0:T(8,128)(2,1)}) %all-gather.4.cloned.1.call-update) | async-done | bytes 8388624 | tf_op jit(solution)/shard_map/all_gather | solution.py:104
  460.7 6.5 %gather_fusion.1 = bf16[64,256,128]{2,1,0:T(8,128)(2,1)} fusion(bf16[128,256,128]{2,1,0:T(8,128)(2,1)} %all-gather.4.cloned.1.call-done, s32[1024]{0:T(1024)S(1)} %pad_clamp_fusion), kind=kCustom, calls=%fused_computation.1 | custom fusion | bytes 8388864 | tf_op jit(solution)/shard_map/jit(_take)/gather | solution.py:105
  467.2 4.6 broadcast_select_fusion
  (9 shorter events, 0.1 us)
Async XLA Ops:
  7.2 270.5 %reduce-scatter.2.cloned.1.call-start = ((), (), s32[]{:S(2)}) async-start(), calls=%async_computation.1 | async-start | bytes 17301504 | tf_op jit(solution)/shard_map/reduce_scatter | solution.py:90
  31.7 245.9 %copy-start = (f32[1,4,256,128]{3,2,1,0:T(8,128)S(1)}, f32[1,4,256,128]{3,2,1,0:T(8,128)}, u32[]{:S(2)}) copy-start(f32[1,4,256,128]{3,2,1,0:T(8,128)} %param.6) | copy-start | bytes 1572868
  31.8 304.8 %all-gather.6.cloned.1.call-start = ((), (), s32[]{:S(2)}) async-start(), calls=%async_computation.3 | async-start | bytes 9437184 | tf_op jit(solution)/shard_map/all_gather | solution.py:48
  281.0 179.8 %all-gather.4.cloned.1.call-start = ((), (), s32[]{:S(2)}) async-start(), calls=%async_computation.2 | async-start | bytes 8650752 | tf_op jit(solution)/shard_map/all_gather | solution.py:104
  340.6 6.6 %copy-start.1 = (f32[4,256,128]{2,1,0:T(8,128)S(1)}, f32[4,256,128]{2,1,0:T(8,128)}, u32[]{:S(2)}) copy-start(f32[4,256,128]{2,1,0:T(8,128)} %reduce-scatter.2.cloned.1.call-done) | copy-start | bytes 1572868
  355.6 6.1 %copy-start.2 = (f32[1,4,256,128]{3,2,1,0:T(8,128)S(1)}, f32[1,4,256,128]{3,2,1,0:T(8,128)}, u32[]{:S(2)}) copy-start(f32[1,4,256,128]{3,2,1,0:T(8,128)} %param.7) | copy-start | bytes 1572868
  356.9 6.8 %copy-start.3 = (s32[64,1]{0,1:T(1,128)S(1)}, s32[64,1]{0,1:T(1,128)}, u32[]{:S(2)}) copy-start(s32[64,1]{0,1:T(1,128)} %param.5) | copy-start | bytes 772
Sparse Core Ops, SparseCore 0:
  31.9 245.7 reduce-scatter.1
  281.1 55.4 all-gather.5
  363.9 96.8 all-gather.3
